TPU v7x, 512 devices: a whole 4x4x16 slice. The times are simulated.
512 devices in a mesh: dp: 4 (over z_hi, core), wide: 16 (over y, x), narrow: 8 (over z_lo).
Axes of the slice: x: 4, y: 4, z: 16 (z_hi: 2, z_lo: 8; z = z_hi * 8 + z_lo), core: 2. Of those that a mesh axis runs over, the one named last changes fastest.
Arguments:
- patches: bfloat16 [1024, 4, 6144], P('wide', 'dp'), parts along dimension 1, may hold values from -6 to 6
- vit_gain: float32 [6144], replicated, may hold values from 0.1 to 1.9
- vit_qkv: bfloat16 [6144, 3, 32, 128], P('narrow', None, 'wide'), may hold values from -4 to 4
- vit_in: bfloat16 [6144, 12288], P('narrow', 'wide'), may hold values from -0.078125 to 0.078125
- vit_attn_out: bfloat16 [4096, 6144], P('wide', 'narrow'), may hold values from -1 to 1
- vit_mlp_out: bfloat16 [12288, 6144], P('wide', 'narrow'), may hold values from -0.109375 to 0.109375
- proj: bfloat16 [6144, 4096], P('narrow', 'wide'), may hold values from -0.01953125 to 0.01953125
Outputs:
- encoded: bfloat16 [1024, 4, 4096], P('wide', 'dp', 'narrow'), parts along dimension 1
There are 4 independent parts, one for each index of `dp`. A program takes and returns all parts, laid end to end along the dimension named above; an argument that names none is the same for every part. Nothing has to cross between parts.
All inputs are finite; a program needn't handle non-finite values.
Results may differ from a plain program's by a relative error of at most 0.035.
Values may be sent and summed in bfloat16 or wider, within the bound.
No kernel may reach another device: no remote copies, remote signals or barrier semaphores. Data moves between devices by JAX's collectives and lax.ppermute only.
A program may use at most 64 MiB of HBM per device.

v0:
```python
import math

import jax
import jax.numpy as jnp
from jax import lax
from jax.sharding import PartitionSpec as P


def layer_norm(inputs, gain_row):
    widened = inputs.astype(jnp.float32)
    centred = widened - jnp.mean(widened, axis=-1, keepdims=True)
    variance = jnp.mean(centred * centred, axis=-1, keepdims=True)
    return (centred * lax.rsqrt(variance + 1e-06) * gain_row).astype(jnp.bfloat16)


def attend(queries, keys_all, values_all):
    score_scale = 1.0 / math.sqrt(queries.shape[-1])
    scores = (
        jnp.einsum("pihd,qihd->ihpq", queries, keys_all, preferred_element_type=jnp.float32)
        * score_scale
    )
    highest = jnp.max(scores, axis=-1, keepdims=True)
    exponentials = jnp.exp(scores - highest)
    totals = jnp.sum(exponentials, axis=-1)
    weights = exponentials.astype(jnp.bfloat16)
    mixed_sum = jnp.einsum(
        "ihpq,qihd->pihd", weights, values_all, preferred_element_type=jnp.float32
    )
    return (mixed_sum / jnp.transpose(totals, (2, 0, 1))[..., None]).astype(jnp.bfloat16)


def per_device(patches, vit_gain, vit_qkv, vit_in, vit_attn_out, vit_mlp_out, proj):
    local_rows = patches.shape[0]
    images = patches.shape[1]
    feature_block = vit_in.shape[0]
    heads_here = vit_qkv.shape[2]
    head_width = vit_qkv.shape[3]
    qkv_cols = 3 * heads_here * head_width
    narrow_start = lax.axis_index("narrow") * feature_block
    normed = layer_norm(patches, vit_gain)
    normed_part = lax.dynamic_slice_in_dim(normed, narrow_start, feature_block, 2)
    in_weight = jnp.concatenate([vit_qkv.reshape(feature_block, qkv_cols), vit_in], axis=1)
    piece_rows = lax.all_gather(normed_part, "wide", axis=0, tiled=True)
    flat_rows = piece_rows.reshape(-1, feature_block)
    joined = jnp.dot(flat_rows, in_weight, preferred_element_type=jnp.float32)
    partial_in = joined.reshape(piece_rows.shape[0], images, -1)
    summed_in = lax.psum(partial_in.astype(jnp.bfloat16), "narrow").astype(jnp.float32)
    row_count = summed_in.shape[0]
    qkv_all = (
        summed_in[..., :qkv_cols]
        .astype(jnp.bfloat16)
        .reshape(row_count, images, 3, heads_here, head_width)
    )
    activated = jax.nn.gelu(summed_in[..., qkv_cols:], approximate=False).astype(jnp.bfloat16)
    qkv_all, act_rows = (qkv_all, activated)
    mixed_heads = attend(qkv_all[:, :, 0], qkv_all[:, :, 1], qkv_all[:, :, 2])
    mixed_rows = mixed_heads.reshape(mixed_heads.shape[0], images, heads_here * head_width)
    heads_rows = mixed_rows.reshape(lax.axis_size("wide") * local_rows * images, -1)
    units_rows = act_rows.reshape(lax.axis_size("wide") * local_rows * images, -1)
    branch_terms = jnp.dot(heads_rows, vit_attn_out, preferred_element_type=jnp.float32)
    branch_terms = branch_terms + jnp.dot(
        units_rows, vit_mlp_out, preferred_element_type=jnp.float32
    )
    branch_sum = lax.psum_scatter(
        branch_terms.reshape(lax.axis_size("wide") * local_rows, images, -1).astype(jnp.bfloat16),
        "wide",
        scatter_dimension=0,
        tiled=True,
    ).astype(jnp.float32)
    own_columns = lax.dynamic_slice_in_dim(patches, narrow_start, feature_block, 2)
    vit_output = (own_columns.astype(jnp.float32) + branch_sum).astype(jnp.bfloat16)
    flat_output = vit_output.reshape(local_rows * images, feature_block)
    partial_encoded = jnp.dot(
        flat_output,
        lax.all_gather(proj, "wide", axis=1, tiled=True),
        preferred_element_type=jnp.float32,
    ).reshape(local_rows, images, -1)
    encoded = lax.psum_scatter(
        partial_encoded.astype(jnp.bfloat16), "narrow", scatter_dimension=2, tiled=True
    )
    return encoded


def solution(mesh):
    return jax.shard_map(
        per_device,
        mesh=mesh,
        in_specs=(
            P("wide", "dp", None),
            P(),
            P("narrow", None, "wide", None),
            P("narrow", "wide"),
            P("wide", "narrow"),
            P("wide", "narrow"),
            P("narrow", "wide"),
        ),
        out_specs=P("wide", "dp", "narrow"),
        check_vma=False,
    )
```

profile of v0, /device:TPU:480, one launch (start us, length us, event | category | flops | bytes accessed | tf_op | source)
XLA Modules:
  0.0 509.6 jit_solution(944441990527074840)
XLA Ops:
  6.5 0.0 copy-start
  6.5 0.0 all-gather.3.cloned.1.call-start
  6.5 1.4 convert_reduce_fusion
  8.0 1.5 multiply_reduce_fusion.1
  9.5 0.8 dynamic-slice
  10.3 0.7 fusion.86
  11.0 0.0 all-gather.3.cloned.1.call-update
  11.0 0.0 all-reduce.2.cloned.1.call-start
  11.1 3.1 reshape.76
  14.2 55.0 %all-gather.3.cloned.1.call-done = bf16[1024,1,768]{2,0,1:T(8,128)(2,1)} async-done(((bf16[64,1,768]{2,0,1:T(8,128)(2,1)}), bf16[1024,1,768]{2,0,1:T(8,128)(2,1)}) %all-gather.3.cloned.1.call-update) | async-done | bytes 1572880 | tf_op jit(solution)/shard_map/all_gather | solution.py:43
  69.2 6.0 %fusion.7 = bf16[1024,1,1536]{2,0,1:T(8,128)(2,1)} fusion(bf16[768,768]{1,0:T(8,128)(2,1)} %param.10, bf16[768,768]{1,0:T(8,128)(2,1)S(1)} %reshape.76, bf16[1024,1,768]{2,0,1:T(8,128)(2,1)} %all-gather.3.cloned.1.call-done), kind=kOutput, calls=%fused_computation.13 | convolution fusion | flops 2422210560 | bytes 7077888 | tf_op jit(solution)/shard_map/dot_general | solution.py:45
  75.3 0.0 all-reduce.2.cloned.1.call-update
  75.3 0.0 reduce-scatter.3.cloned.1.call-start
  75.3 165.0 %all-reduce.2.cloned.1.call-done = bf16[1024,1,1536]{2,0,1:T(8,128)(2,1)} async-done(((bf16[1024,1,1536]{2,0,1:T(8,128)(2,1)}), bf16[1024,1,1536]{2,0,1:T(8,128)(2,1)}) %all-reduce.2.cloned.1.call-update) | async-done | bytes 3145744 | tf_op jit(solution)/shard_map/psum | solution.py:47
  240.4 2.7 slice.25
  243.0 3.3 reshape.77
  246.4 2.1 fusion.123
  248.5 0.6 copy.13
  249.1 2.5 multiply_reduce_fusion
  251.5 1.4 fusion
  252.9 0.0 copy-start.1
  252.9 1.7 divide_convert_fusion
  254.6 0.0 copy-done
  254.6 0.2 copy-done.1
  254.8 0.0 copy-start.2
  254.8 7.8 %fusion.43 = f32[1024,768]{1,0:T(8,128)S(1)} fusion(bf16[768,768]{1,0:T(8,128)(2,1)S(1)} %copy-done, bf16[1024,1,1536]{2,0,1:T(8,128)(2,1)S(1)} %copy-done.1), kind=kOutput, calls=%fused_computation.52 | convolution fusion | flops 1259864064 | bytes 5898240 | tf_op jit(solution)/shard_map/dot_general | solution.py:61
  262.6 0.0 copy-done.2
  262.6 1.8 fusion.77
  264.4 0.0 reduce-scatter.3.cloned.1.call-update
  264.4 0.0 all-gather.5.cloned.1.call-start
  264.5 0.5 all-gather.5.cloned.1.call-update
  265.0 0.0 reduce-scatter.5.cloned.1.call-start
  265.1 84.9 %reduce-scatter.3.cloned.1.call-done = bf16[64,1,768]{2,0,1:T(8,128)(2,1)} async-done(((bf16[1024,1,768]{2,0,1:T(8,128)(2,1)}), bf16[64,1,768]{2,0,1:T(8,128)(2,1)}) %reduce-scatter.3.cloned.1.call-update) | async-done | bytes 98320 | tf_op jit(solution)/shard_map/reduce_scatter | solution.py:64
  350.0 84.6 %all-gather.5.cloned.1.call-done = bf16[768,4096]{1,0:T(8,128)(2,1)} async-done(((bf16[768,256]{1,0:T(8,128)(2,1)}), bf16[768,4096]{1,0:T(8,128)(2,1)}) %all-gather.5.cloned.1.call-update) | async-done | bytes 6291472 | tf_op jit(solution)/shard_map/all_gather | solution.py:75
  434.6 4.9 fusion.2
  439.5 0.0 reduce-scatter.5.cloned.1.call-update
  439.5 63.5 %reduce-scatter.5.cloned.1.call-done = bf16[64,1,512]{2,0,1:T(8,128)(2,1)} async-done(((bf16[64,1,4096]{2,0,1:T(8,128)(2,1)}), bf16[64,1,512]{2,0,1:T(8,128)(2,1)}) %reduce-scatter.5.cloned.1.call-update) | async-done | bytes 65552 | tf_op jit(solution)/shard_map/reduce_scatter | solution.py:78
  (2 shorter events, 0.0 us)
Async XLA Ops:
  6.5 248.1 %copy-start = (bf16[768,768]{1,0:T(8,128)(2,1)S(1)}, bf16[768,768]{1,0:T(8,128)(2,1)}, u32[]{:S(2)}) copy-start(bf16[768,768]{1,0:T(8,128)(2,1)} %param.12) | copy-start | bytes 3538948
  6.5 62.7 %all-gather.3.cloned.1.call-start = ((), (), s32[]{:S(2)}) async-start(), calls=%async_computation.2 | async-start | bytes 1671168 | tf_op jit(solution)/shard_map/all_gather | solution.py:43
  11.0 229.3 %all-reduce.2.cloned.1.call-start = ((), (), s32[]{:S(2)}) async-start(), calls=%async_computation.3 | async-start | bytes 6291456 | tf_op jit(solution)/shard_map/psum | solution.py:47
  75.3 274.7 %reduce-scatter.3.cloned.1.call-start = ((), (), s32[]{:S(2)}) async-start(), calls=%async_computation.4 | async-start | bytes 1671168 | tf_op jit(solution)/shard_map/reduce_scatter | solution.py:64
  252.9 1.9 copy-start.1
  254.8 7.8 %copy-start.2 = (bf16[256,768]{1,0:T(8,128)(2,1)S(1)}, bf16[256,768]{1,0:T(8,128)(2,1)}, u32[]{:S(2)}) copy-start(bf16[256,768]{1,0:T(8,128)(2,1)} %param.11) | copy-start | bytes 1179652
  264.4 170.1 %all-gather.5.cloned.1.call-start = ((), (), s32[]{:S(2)}) async-start(), calls=%async_computation.5 | async-start | bytes 6684672 | tf_op jit(solution)/shard_map/all_gather | solution.py:75
  265.0 238.0 %reduce-scatter.5.cloned.1.call-start = ((), (), s32[]{:S(2)}) async-start(), calls=%async_computation.6 | async-start | bytes 589824 | tf_op jit(solution)/shard_map/reduce_scatter | solution.py:78
Sparse Core Ops, SparseCore 0:
  11.2 58.0 all-gather.2
  75.4 164.9 all-reduce.1
  264.6 85.3 reduce-scatter.2
  352.8 81.7 all-gather.4
  439.6 63.3 reduce-scatter.4
where the time goes:
time: 517 us; the launch traced here: 510 us
  waiting for transfers between devices  454 us (88%)
  matrix products  24.7 us (5%)
  between operations  13.2 us (3%)
  local copies, waits for them, and re-layouts  12.8 us (2%)
    psum x1, waiting for transfers between devices, per_device(): lax.psum(partial_in.astype(jnp.bfloat16), 'narrow').astype(jnp.float32)  165 us
    reduce_scatter x1, waiting for transfers between devices, per_device(): lax.psum_scatter(branch_terms.reshape(lax.axis_size('wide') * local_rows,...  84.9 us
    all_gather x1, waiting for transfers between devices, per_device(): lax.all_gather(proj, 'wide', axis=1, tiled=True)  84.6 us
    reduce_scatter x1, waiting for transfers between devices, per_device(): lax.psum_scatter(partial_encoded.astype(jnp.bfloat16), 'narrow', scatter_...  63.5 us
    all_gather x1, waiting for transfers between devices, per_device(): piece_rows = lax.all_gather(normed_part, 'wide', axis=0, tiled=True)  55 us
  transfers between devices with their start and end apart: 5, of which 5 were waited for; matrix products, arithmetic and copies ran while one was open for 1% of the time, Pallas kernels for 0%

commit v1 on v0

v1 whole, which is shorter than its diff:
```python
import math

import jax
import jax.numpy as jnp
from jax import lax
from jax.sharding import PartitionSpec as P


def layer_norm(inputs, gain_row):
    widened = inputs.astype(jnp.float32)
    centred = widened - jnp.mean(widened, axis=-1, keepdims=True)
    variance = jnp.mean(centred * centred, axis=-1, keepdims=True)
    return (centred * lax.rsqrt(variance + 1e-06) * gain_row).astype(jnp.bfloat16)


def attend(queries, keys_all, values_all):
    score_scale = 1.0 / math.sqrt(queries.shape[-1])
    scores = (
        jnp.einsum("pihd,qihd->ihpq", queries, keys_all, preferred_element_type=jnp.float32)
        * score_scale
    )
    highest = jnp.max(scores, axis=-1, keepdims=True)
    exponentials = jnp.exp(scores - highest)
    totals = jnp.sum(exponentials, axis=-1)
    weights = exponentials.astype(jnp.bfloat16)
    mixed_sum = jnp.einsum(
        "ihpq,qihd->pihd", weights, values_all, preferred_element_type=jnp.float32
    )
    return (mixed_sum / jnp.transpose(totals, (2, 0, 1))[..., None]).astype(jnp.bfloat16)


def gather_wide(block, n_wide):
    spread = jnp.broadcast_to(block[None], (n_wide,) + block.shape)
    got = lax.all_to_all(spread, "wide", 0, 0, tiled=True)
    return got.reshape((n_wide * block.shape[0],) + block.shape[1:])


def scatter_sum(terms, axis_name, parts):
    got = lax.all_to_all(terms.astype(jnp.bfloat16), axis_name, 0, 0, tiled=True)
    got = got.reshape((parts, terms.shape[0] // parts) + terms.shape[1:])
    return jnp.sum(got.astype(jnp.float32), axis=0)


def per_device(patches, vit_gain, vit_qkv, vit_in, vit_attn_out, vit_mlp_out, proj):
    n_wide = lax.axis_size("wide")
    n_narrow = lax.axis_size("narrow")
    w = lax.axis_index("wide")
    n = lax.axis_index("narrow")
    local_rows = patches.shape[0]
    images = patches.shape[1]
    flat_local = local_rows * images
    feature_block = vit_in.shape[0]
    heads_here = vit_qkv.shape[2]
    head_width = vit_qkv.shape[3]
    qkv_cols = 3 * heads_here * head_width
    narrow_start = n * feature_block
    normed = layer_norm(patches, vit_gain)
    normed_part = lax.dynamic_slice_in_dim(normed, narrow_start, feature_block, 2)
    in_weight = jnp.concatenate([vit_qkv.reshape(feature_block, qkv_cols), vit_in], axis=1)
    flat_rows = gather_wide(normed_part.reshape(flat_local, feature_block), n_wide)
    joined = jnp.dot(flat_rows, in_weight, preferred_element_type=jnp.float32)
    row_count = n_wide * local_rows
    partial_in = joined.reshape(row_count, images, -1)
    summed_in = lax.psum(partial_in.astype(jnp.bfloat16), "narrow").astype(jnp.float32)
    qkv_all = (
        summed_in[..., :qkv_cols]
        .astype(jnp.bfloat16)
        .reshape(row_count, images, 3, heads_here, head_width)
    )
    activated = jax.nn.gelu(summed_in[..., qkv_cols:], approximate=False).astype(jnp.bfloat16)
    mixed_heads = attend(qkv_all[:, :, 0], qkv_all[:, :, 1], qkv_all[:, :, 2])
    heads_rows = mixed_heads.reshape(row_count * images, heads_here * head_width)
    units_rows = activated.reshape(row_count * images, -1)
    branch_terms = jnp.dot(heads_rows, vit_attn_out, preferred_element_type=jnp.float32)
    branch_terms = branch_terms + jnp.dot(
        units_rows, vit_mlp_out, preferred_element_type=jnp.float32
    )
    branch_sum = scatter_sum(branch_terms, "wide", n_wide)
    own_columns = lax.dynamic_slice_in_dim(patches, narrow_start, feature_block, 2)
    vit_output = (
        own_columns.reshape(flat_local, feature_block).astype(jnp.float32) + branch_sum
    ).astype(jnp.bfloat16)
    output_rows = gather_wide(vit_output, n_wide)
    partial_encoded = jnp.dot(output_rows, proj, preferred_element_type=jnp.float32)
    encoded_piece = scatter_sum(partial_encoded, "narrow", n_narrow).astype(jnp.bfloat16)
    ratio = n_wide // n_narrow
    enc_block = proj.shape[1]
    pieces = encoded_piece.reshape(ratio, flat_local, enc_block)
    columns = []
    for i in range(ratio):
        got = None
        for j in range(ratio):
            pairs = [
                (src_w * n_narrow + src_n, (ratio * src_n + j) * n_narrow + src_w // ratio)
                for src_w in range(i, n_wide, ratio)
                for src_n in range(n_narrow)
            ]
            moved = lax.ppermute(pieces[j], ("wide", "narrow"), pairs)
            got = moved if got is None else jnp.where(w % ratio == j, moved, got)
        columns.append(got)
    encoded = jnp.concatenate(columns, axis=1)
    return encoded.reshape(local_rows, images, ratio * enc_block)


def solution(mesh):
    return jax.shard_map(
        per_device,
        mesh=mesh,
        in_specs=(
            P("wide", "dp", None),
            P(),
            P("narrow", None, "wide", None),
            P("narrow", "wide"),
            P("wide", "narrow"),
            P("wide", "narrow"),
            P("narrow", "wide"),
        ),
        out_specs=P("wide", "dp", "narrow"),
        check_vma=False,
    )
```

time: 517 us -> 361 us (0.70)
  the two profiles are of different devices: /device:TPU:480 before, /device:TPU:30 now
where the time goes in v1:
time: 361 us; the launch traced here: 360 us
  waiting for transfers between devices  200 us (55%)
  blocking collectives  79.4 us (22%)
  starting transfers between devices  27.2 us (8%)
  matrix products  19 us (5%)
  local copies, waits for them, and re-layouts  15 us (4%)
  between operations  13.6 us (4%)
  other arithmetic  6.28 us (2%)
    psum x1, waiting for transfers between devices, per_device(): lax.psum(partial_in.astype(jnp.bfloat16), 'narrow').astype(jnp.float32)  171 us
    all_to_all x2, blocking collectives, scatter_sum(): lax.all_to_all(terms.astype(jnp.bfloat16), axis_name, 0, 0, tiled=True)  54.6 us
    all_to_all x1, blocking collectives, gather_wide(): got = lax.all_to_all(spread, 'wide', 0, 0, tiled=True)  24.8 us
    ppermute x4, starting transfers between devices, per_device(): moved = lax.ppermute(pieces[j], ('wide', 'narrow'), pairs)  18.1 us
    ppermute x4, waiting for transfers between devices, per_device(): moved = lax.ppermute(pieces[j], ('wide', 'narrow'), pairs)  15.3 us
    all_to_all x1, waiting for transfers between devices, gather_wide(): got = lax.all_to_all(spread, 'wide', 0, 0, tiled=True)  13.4 us
    all_to_all x1, starting transfers between devices, gather_wide(): got = lax.all_to_all(spread, 'wide', 0, 0, tiled=True)  9.07 us
    dot_general x1, matrix products, per_device(): jnp.dot(units_rows, vit_mlp_out, preferred_element_type=jnp.float32)  8.04 us
  transfers between devices with their start and end apart: 6, of which 4 were waited for; matrix products, arithmetic and copies ran while one was open for 1% of the time, Pallas kernels for 0%

profile of v1, /device:TPU:30, one launch (start us, length us, event | category | flops | bytes accessed | tf_op | source)
XLA Modules:
  0.0 360.5 jit_solution(112845400811873960)
XLA Ops:
  6.5 0.0 copy-start
  6.5 1.4 convert_reduce_fusion.1
  8.0 1.5 multiply_reduce_fusion.1
  9.5 0.8 dynamic-slice
  10.3 0.1 fusion.85
  10.4 1.3 broadcast_in_dim.7
  11.7 9.1 %all-to-all-start = ((bf16[16,64,768]{2,1,0:T(8,128)(2,1)}), bf16[16,64,768]{2,1,0:T(8,128)(2,1)S(1)}, u32[]{:S(2)}, u32[]{:S(2)}) async-start(bf16[16,64,768]{2,1,0:T(8,128)(2,1)} %broadcast_in_dim.7), calls=%async_computation | async-start | bytes 3145728 | tf_op jit(solution)/shard_map/all_to_all | solution.py:34
  20.8 0.0 all-reduce.2.cloned.1.call-start
  20.8 3.9 %reshape.104 = bf16[768,768]{1,0:T(8,128)(2,1)} reshape(bf16[768,3,2,128]{3,2,1,0:T(2,128)(2,1)} %param.9) | data formatting | bytes 2359296 | tf_op jit(solution)/shard_map/reshape | solution.py:59
  24.7 13.4 %all-to-all-done = bf16[16,64,768]{2,1,0:T(8,128)(2,1)S(1)} async-done(((bf16[16,64,768]{2,1,0:T(8,128)(2,1)}), bf16[16,64,768]{2,1,0:T(8,128)(2,1)S(1)}, u32[]{:S(2)}, u32[]{:S(2)}) %all-to-all-start) | async-done | bytes 1572896 | tf_op jit(solution)/shard_map/all_to_all | solution.py:34
  38.1 5.6 %fusion.6 = bf16[1024,1,1536]{2,0,1:T(8,128)(2,1)} fusion(bf16[1024,768]{1,0:T(8,128)(2,1)S(1)} %bitcast.50, bf16[768,768]{1,0:T(8,128)(2,1)} %param.10, bf16[768,768]{1,0:T(8,128)(2,1)} %reshape.104), kind=kOutput, calls=%fused_computation.11 | convolution fusion | flops 2422210560 | bytes 7077888 | tf_op jit(solution)/shard_map/dot_general | solution.py:61
  43.7 0.0 all-reduce.2.cloned.1.call-update
  43.7 171.2 %all-reduce.2.cloned.1.call-done = bf16[1024,1,1536]{2,0,1:T(8,128)(2,1)} async-done(((bf16[1024,1,1536]{2,0,1:T(8,128)(2,1)}), bf16[1024,1,1536]{2,0,1:T(8,128)(2,1)}) %all-reduce.2.cloned.1.call-update) | async-done | bytes 3145744 | tf_op jit(solution)/shard_map/psum | solution.py:64
  215.0 2.6 slice.37
  217.6 3.3 reshape.105
  221.0 2.1 fusion.118
  223.0 0.6 copy.13
  223.6 2.5 multiply_reduce_fusion
  226.1 1.4 fusion
  227.5 0.0 copy-start.1
  227.5 1.7 divide_convert_fusion
  229.2 0.0 copy-done
  229.2 0.2 copy-done.1
  229.4 0.0 copy-start.2
  229.4 8.0 %fusion.42 = f32[1024,768]{1,0:T(8,128)S(1)} fusion(bf16[768,768]{1,0:T(8,128)(2,1)S(1)} %copy-done, bf16[1024,1,1536]{2,0,1:T(8,128)(2,1)S(1)} %copy-done.1), kind=kOutput, calls=%fused_computation.51 | convolution fusion | flops 1259864064 | bytes 5898240 | tf_op jit(solution)/shard_map/dot_general | solution.py:75
  237.4 0.0 copy-done.2
  237.5 0.6 add_convert_fusion
  238.1 25.2 %all_to_all.28 = bf16[16,64,768]{2,1,0:T(8,128)(2,1)S(1)} all-to-all(bf16[16,64,768]{2,1,0:T(8,128)(2,1)S(1)} %bitcast.49), channel_id=1, replica_groups=mesh['dp'=4,'wide'=16,'narrow'=8] {'wide'}, dimensions={0} | all-to-all | bytes 3145728 | tf_op jit(solution)/shard_map/all_to_all | solution.py:39
  263.3 0.0 copy-start.3
  263.3 0.2 convert_reduce_fusion
  263.5 0.9 fusion.84
  264.4 0.1 broadcast_in_dim.8
  264.6 24.8 %all_to_all.29 = bf16[16,64,768]{2,1,0:T(8,128)(2,1)S(1)} all-to-all(bf16[16,64,768]{2,1,0:T(8,128)(2,1)S(1)} %broadcast_in_dim.8), channel_id=1, replica_groups=mesh['dp'=4,'wide'=16,'narrow'=8] {'wide'}, dimensions={0} | all-to-all | bytes 3145728 | tf_op jit(solution)/shard_map/all_to_all | solution.py:34
  289.4 0.0 copy-done.3
  289.4 0.6 convolution_convert_fusion.1
  290.0 29.4 %all_to_all.30 = bf16[8,128,256]{2,1,0:T(8,128)(2,1)S(1)} all-to-all(bf16[8,128,256]{2,1,0:T(8,128)(2,1)S(1)} %bitcast.52), channel_id=1, replica_groups=mesh['dp'=4,'wide'=16,'narrow'=8] {'narrow'}, dimensions={0} | all-to-all | bytes 1048576 | tf_op jit(solution)/shard_map/all_to_all | solution.py:39
  319.4 0.1 reduce_sum.55
  319.5 8.5 %collective-permute-start.3 = (bf16[64,256]{1,0:T(8,128)(2,1)S(1)}, bf16[64,256]{1,0:T(8,128)(2,1)S(1)}, u32[]{:S(2)}, u32[]{:S(2)}) collective-permute-start(bf16[64,256]{1,0:T(8,128)(2,1)S(1)} %get-tuple-element.10), channel_id=1, source_target_pairs={{8,0},{9,16},{10,32},{11,48},{12,64},{13,80},{14,96},{15,112},{24,... | collective-permute-start | bytes 98312 | tf_op jit(solution)/shard_map/ppermute | solution.py:98
  328.0 7.6 %collective-permute-start.2 = (bf16[64,256]{1,0:T(8,128)(2,1)S(1)}, bf16[64,256]{1,0:T(8,128)(2,1)S(1)}, u32[]{:S(2)}, u32[]{:S(2)}) collective-permute-start(bf16[64,256]{1,0:T(8,128)(2,1)S(1)} %get-tuple-element.11), channel_id=1, source_target_pairs={{8,8},{9,24},{10,40},{11,56},{12,72},{13,88},{14,104},{15,120},{24... | collective-permute-start | bytes 98312 | tf_op jit(solution)/shard_map/ppermute | solution.py:98
  335.7 0.7 collective-permute-start.1
  336.3 1.3 collective-permute-start
  337.6 0.0 collective-permute-done.3
  337.6 7.5 %collective-permute-done.2 = bf16[64,256]{1,0:T(8,128)(2,1)S(1)} collective-permute-done((bf16[64,256]{1,0:T(8,128)(2,1)S(1)}, bf16[64,256]{1,0:T(8,128)(2,1)S(1)}, u32[]{:S(2)}, u32[]{:S(2)}) %collective-permute-start.2) | collective-permute-done | bytes 32800 | tf_op jit(solution)/shard_map/ppermute | solution.py:98
  345.1 0.0 collective-permute-done.1
  345.1 7.9 %collective-permute-done = bf16[64,256]{1,0:T(8,128)(2,1)S(1)} collective-permute-done((bf16[64,256]{1,0:T(8,128)(2,1)S(1)}, bf16[64,256]{1,0:T(8,128)(2,1)S(1)}, u32[]{:S(2)}, u32[]{:S(2)}) %collective-permute-start) | collective-permute-done | bytes 32800 | tf_op jit(solution)/shard_map/ppermute | solution.py:98
  353.0 0.6 maximum_bitcast_fusion
  (5 shorter events, 0.0 us)
Async XLA Ops:
  6.5 222.7 %copy-start = (bf16[768,768]{1,0:T(8,128)(2,1)S(1)}, bf16[768,768]{1,0:T(8,128)(2,1)}, u32[]{:S(2)}) copy-start(bf16[768,768]{1,0:T(8,128)(2,1)} %param.12) | copy-start | bytes 3538948
  11.7 26.4 %all-to-all-start = ((bf16[16,64,768]{2,1,0:T(8,128)(2,1)}), bf16[16,64,768]{2,1,0:T(8,128)(2,1)S(1)}, u32[]{:S(2)}, u32[]{:S(2)}) async-start(bf16[16,64,768]{2,1,0:T(8,128)(2,1)} %broadcast_in_dim.7), calls=%async_computation | async-start | bytes 3145728 | tf_op jit(solution)/shard_map/all_to_all | solution.py:34
  20.8 194.2 %all-reduce.2.cloned.1.call-start = ((), (), s32[]{:S(2)}) async-start(), calls=%async_computation.4 | async-start | bytes 6291456 | tf_op jit(solution)/shard_map/psum | solution.py:64
  227.5 1.9 copy-start.1
  229.4 8.1 %copy-start.2 = (bf16[256,768]{1,0:T(8,128)(2,1)S(1)}, bf16[256,768]{1,0:T(8,128)(2,1)}, u32[]{:S(2)}) copy-start(bf16[256,768]{1,0:T(8,128)(2,1)} %param.11) | copy-start | bytes 1179652
  263.3 26.2 %copy-start.3 = (bf16[768,256]{1,0:T(8,128)(2,1)S(1)}, bf16[768,256]{1,0:T(8,128)(2,1)}, u32[]{:S(2)}) copy-start(bf16[768,256]{1,0:T(8,128)(2,1)} %param.13) | copy-start | bytes 1179652
  319.5 18.1 %collective-permute-start.3 = (bf16[64,256]{1,0:T(8,128)(2,1)S(1)}, bf16[64,256]{1,0:T(8,128)(2,1)S(1)}, u32[]{:S(2)}, u32[]{:S(2)}) collective-permute-start(bf16[64,256]{1,0:T(8,128)(2,1)S(1)} %get-tuple-element.10), channel_id=1, source_target_pairs={{8,0},{9,16},{10,32},{11,48},{12,64},{13,80},{14,96},{15,112},{24,... | collective-permute-start | bytes 98312 | tf_op jit(solution)/shard_map/ppermute | solution.py:98
  328.0 17.1 %collective-permute-start.2 = (bf16[64,256]{1,0:T(8,128)(2,1)S(1)}, bf16[64,256]{1,0:T(8,128)(2,1)S(1)}, u32[]{:S(2)}, u32[]{:S(2)}) collective-permute-start(bf16[64,256]{1,0:T(8,128)(2,1)S(1)} %get-tuple-element.11), channel_id=1, source_target_pairs={{8,8},{9,24},{10,40},{11,56},{12,72},{13,88},{14,104},{15,120},{24... | collective-permute-start | bytes 98312 | tf_op jit(solution)/shard_map/ppermute | solution.py:98
  335.7 9.4 %collective-permute-start.1 = (bf16[64,256]{1,0:T(8,128)(2,1)S(1)}, bf16[64,256]{1,0:T(8,128)(2,1)S(1)}, u32[]{:S(2)}, u32[]{:S(2)}) collective-permute-start(bf16[64,256]{1,0:T(8,128)(2,1)S(1)} %get-tuple-element.10), channel_id=1, source_target_pairs={{0,0},{1,16},{2,32},{3,48},{4,64},{5,80},{6,96},{7,112},{16,1},{17... | collective-permute-start | bytes 98312 | tf_op jit(solution)/shard_map/ppermute | solution.py:98
  336.3 16.6 %collective-permute-start = (bf16[64,256]{1,0:T(8,128)(2,1)S(1)}, bf16[64,256]{1,0:T(8,128)(2,1)S(1)}, u32[]{:S(2)}, u32[]{:S(2)}) collective-permute-start(bf16[64,256]{1,0:T(8,128)(2,1)S(1)} %get-tuple-element.11), channel_id=1, source_target_pairs={{0,8},{1,24},{2,40},{3,56},{4,72},{5,88},{6,104},{7,120},{16,9},{1... | collective-permute-start | bytes 98312 | tf_op jit(solution)/shard_map/ppermute | solution.py:98
Sparse Core Ops, SparseCore 0:
  43.9 171.0 all-reduce.1

commit v2 on v1

--- a/solution.py
+++ b/solution.py
@@ -52,22 +52,22 @@
     feature_block = vit_in.shape[0]
     heads_here = vit_qkv.shape[2]
     head_width = vit_qkv.shape[3]
-    qkv_cols = 3 * heads_here * head_width
     narrow_start = n * feature_block
     normed = layer_norm(patches, vit_gain)
     normed_part = lax.dynamic_slice_in_dim(normed, narrow_start, feature_block, 2)
-    in_weight = jnp.concatenate([vit_qkv.reshape(feature_block, qkv_cols), vit_in], axis=1)
     flat_rows = gather_wide(normed_part.reshape(flat_local, feature_block), n_wide)
-    joined = jnp.dot(flat_rows, in_weight, preferred_element_type=jnp.float32)
     row_count = n_wide * local_rows
-    partial_in = joined.reshape(row_count, images, -1)
-    summed_in = lax.psum(partial_in.astype(jnp.bfloat16), "narrow").astype(jnp.float32)
-    qkv_all = (
-        summed_in[..., :qkv_cols]
-        .astype(jnp.bfloat16)
-        .reshape(row_count, images, 3, heads_here, head_width)
+    qkv_part = jnp.einsum(
+        "rf,fthd->rthd", flat_rows, vit_qkv, preferred_element_type=jnp.float32
+    ).astype(jnp.bfloat16)
+    hidden_part = jnp.dot(flat_rows, vit_in, preferred_element_type=jnp.float32).astype(
+        jnp.bfloat16
     )
-    activated = jax.nn.gelu(summed_in[..., qkv_cols:], approximate=False).astype(jnp.bfloat16)
+    qkv_sum, hidden_sum = lax.psum((qkv_part, hidden_part), "narrow")
+    qkv_all = qkv_sum.reshape(row_count, images, 3, heads_here, head_width)
+    activated = jax.nn.gelu(hidden_sum.astype(jnp.float32), approximate=False).astype(
+        jnp.bfloat16
+    )
     mixed_heads = attend(qkv_all[:, :, 0], qkv_all[:, :, 1], qkv_all[:, :, 2])
     heads_rows = mixed_heads.reshape(row_count * images, heads_here * head_width)
     units_rows = activated.reshape(row_count * images, -1)

time: 361 us -> 350 us (0.970)
  the two profiles are of different devices: /device:TPU:30 before, /device:TPU:480 now
where the time goes in v2:
time: 350 us; the launch traced here: 349 us
  waiting for transfers between devices  176 us (50%)
  blocking collectives  114 us (33%)
  matrix products  19.6 us (6%)
  starting transfers between devices  18.1 us (5%)
  between operations  13.6 us (4%)
  other arithmetic  6.28 us (2%)
    psum x1, waiting for transfers between devices, per_device(): qkv_sum, hidden_sum = lax.psum((qkv_part, hidden_part), 'narrow')  161 us
    all_to_all x2, blocking collectives, scatter_sum(): lax.all_to_all(terms.astype(jnp.bfloat16), axis_name, 0, 0, tiled=True)  59.9 us
    all_to_all x2, blocking collectives, gather_wide(): got = lax.all_to_all(spread, 'wide', 0, 0, tiled=True)  54.5 us
    ppermute x4, starting transfers between devices, per_device(): moved = lax.ppermute(pieces[j], ('wide', 'narrow'), pairs)  18.1 us
    ppermute x4, waiting for transfers between devices, per_device(): moved = lax.ppermute(pieces[j], ('wide', 'narrow'), pairs)  15.3 us
    dot_general x1, matrix products, per_device(): jnp.dot(units_rows, vit_mlp_out, preferred_element_type=jnp.float32)  8.01 us
  transfers between devices with their start and end apart: 5, of which 3 were waited for; matrix products, arithmetic and copies ran while one was open for 0% of the time, Pallas kernels for 0%

profile of v2, /device:TPU:480, one launch (start us, length us, event | category | flops | bytes accessed | tf_op | source)
XLA Modules:
  0.0 349.3 jit_solution(5248851092254605151)
XLA Ops:
  6.5 0.0 copy-start
  6.5 0.0 all-reduce.3.cloned.1.call-start
  6.5 1.4 convert_reduce_fusion.1
  8.0 1.5 multiply_reduce_fusion.1
  9.5 0.8 dynamic-slice
  10.3 0.1 fusion.80
  10.4 0.1 broadcast_in_dim.7
  10.5 29.6 %all_to_all.28 = bf16[16,64,768]{2,1,0:T(8,128)(2,1)S(1)} all-to-all(bf16[16,64,768]{2,1,0:T(8,128)(2,1)S(1)} %broadcast_in_dim.7), channel_id=1, replica_groups=mesh['dp'=4,'wide'=16,'narrow'=8] {'wide'}, dimensions={0} | all-to-all | bytes 3145728 | tf_op jit(solution)/shard_map/all_to_all | solution.py:34
  40.1 0.0 copy-done
  40.1 0.0 copy-start.3
  40.1 2.5 convolution_convert_fusion
  42.7 0.0 copy-done.3
  42.7 2.6 fusion.69
  45.3 0.0 all-reduce.3.cloned.1.call-update
  45.3 160.8 %all-reduce.3.cloned.1.call-done = (bf16[1024,768]{1,0:T(8,128)(2,1)}, bf16[1024,1,3,2,128]{4,0,3,2,1:T(8,128)(2,1)}) async-done(((bf16[1024,768]{1,0:T(8,128)(2,1)}, bf16[1024,1,3,2,128]{4,0,3,2,1:T(8,128)(2,1)}), (bf16[1024,768]{1,0:T(8,128)(2,1)}, bf16[1024,1,3,2,128]{4,0,3,2,1:T(8,128)(2,1)})) %all-reduce.3.cloned.1.call-update) | async-done | bytes 3145744 | tf_op jit(solution)/shard_map/psum | solution.py:66
  206.1 2.5 multiply_reduce_fusion
  208.6 1.4 fusion
  209.9 0.0 copy-start.2
  209.9 0.0 copy-start.4
  210.0 2.9 divide_convert_fusion
  212.8 0.0 copy-done.2
  212.8 0.0 copy-done.4
  212.8 0.0 copy-start.1
  212.9 8.0 %fusion.37 = f32[1024,768]{1,0:T(8,128)S(1)} fusion(bf16[768,768]{1,0:T(8,128)(2,1)S(1)} %copy-done.4, bf16[1024,768]{1,0:T(8,128)(2,1)S(1)} %copy-done.2), kind=kOutput, calls=%fused_computation.47 | convolution fusion | flops 1259864064 | bytes 5898240 | tf_op jit(solution)/shard_map/dot_general | solution.py:75
  220.9 0.0 copy-done.1
  220.9 0.6 add_convert_fusion
  221.5 29.2 %all_to_all.29 = bf16[16,64,768]{2,1,0:T(8,128)(2,1)S(1)} all-to-all(bf16[16,64,768]{2,1,0:T(8,128)(2,1)S(1)} %bitcast.50), channel_id=1, replica_groups=mesh['dp'=4,'wide'=16,'narrow'=8] {'wide'}, dimensions={0} | all-to-all | bytes 3145728 | tf_op jit(solution)/shard_map/all_to_all | solution.py:39
  250.7 0.0 copy-start.5
  250.7 0.2 convert_reduce_fusion
  251.0 0.9 fusion.79
  251.9 0.1 broadcast_in_dim.8
  252.0 24.9 %all_to_all.30 = bf16[16,64,768]{2,1,0:T(8,128)(2,1)S(1)} all-to-all(bf16[16,64,768]{2,1,0:T(8,128)(2,1)S(1)} %broadcast_in_dim.8), channel_id=1, replica_groups=mesh['dp'=4,'wide'=16,'narrow'=8] {'wide'}, dimensions={0} | all-to-all | bytes 3145728 | tf_op jit(solution)/shard_map/all_to_all | solution.py:34
  276.9 0.0 copy-done.5
  276.9 0.6 convolution_convert_fusion.2
  277.5 30.7 %all_to_all.31 = bf16[8,128,256]{2,1,0:T(8,128)(2,1)S(1)} all-to-all(bf16[8,128,256]{2,1,0:T(8,128)(2,1)S(1)} %bitcast.54), channel_id=1, replica_groups=mesh['dp'=4,'wide'=16,'narrow'=8] {'narrow'}, dimensions={0} | all-to-all | bytes 1048576 | tf_op jit(solution)/shard_map/all_to_all | solution.py:39
  308.2 0.1 reduce_sum.55
  308.3 8.2 %collective-permute-start = (bf16[64,256]{1,0:T(8,128)(2,1)S(1)}, bf16[64,256]{1,0:T(8,128)(2,1)S(1)}, u32[]{:S(2)}, u32[]{:S(2)}) collective-permute-start(bf16[64,256]{1,0:T(8,128)(2,1)S(1)} %get-tuple-element.10), channel_id=1, source_target_pairs={{0,8},{1,24},{2,40},{3,56},{4,72},{5,88},{6,104},{7,120},{16,9},{1... | collective-permute-start | bytes 98312 | tf_op jit(solution)/shard_map/ppermute | solution.py:98
  316.5 8.0 %collective-permute-start.1 = (bf16[64,256]{1,0:T(8,128)(2,1)S(1)}, bf16[64,256]{1,0:T(8,128)(2,1)S(1)}, u32[]{:S(2)}, u32[]{:S(2)}) collective-permute-start(bf16[64,256]{1,0:T(8,128)(2,1)S(1)} %get-tuple-element.9), channel_id=1, source_target_pairs={{0,0},{1,16},{2,32},{3,48},{4,64},{5,80},{6,96},{7,112},{16,1},{17... | collective-permute-start | bytes 98312 | tf_op jit(solution)/shard_map/ppermute | solution.py:98
  324.5 0.7 collective-permute-start.2
  325.2 1.3 collective-permute-start.3
  326.5 0.0 collective-permute-done
  326.5 6.9 %collective-permute-done.1 = bf16[64,256]{1,0:T(8,128)(2,1)S(1)} collective-permute-done((bf16[64,256]{1,0:T(8,128)(2,1)S(1)}, bf16[64,256]{1,0:T(8,128)(2,1)S(1)}, u32[]{:S(2)}, u32[]{:S(2)}) %collective-permute-start.1) | collective-permute-done | bytes 32800 | tf_op jit(solution)/shard_map/ppermute | solution.py:98
  333.4 0.0 collective-permute-done.2
  333.4 8.4 %collective-permute-done.3 = bf16[64,256]{1,0:T(8,128)(2,1)S(1)} collective-permute-done((bf16[64,256]{1,0:T(8,128)(2,1)S(1)}, bf16[64,256]{1,0:T(8,128)(2,1)S(1)}, u32[]{:S(2)}, u32[]{:S(2)}) %collective-permute-start.3) | collective-permute-done | bytes 32800 | tf_op jit(solution)/shard_map/ppermute | solution.py:98
  341.8 0.6 maximum_bitcast_fusion
  (5 shorter events, 0.0 us)
Async XLA Ops:
  6.5 33.6 %copy-start = (bf16[768,768]{1,0:T(8,128)(2,1)S(1)}, bf16[768,768]{1,0:T(8,128)(2,1)}, u32[]{:S(2)}) copy-start(bf16[768,768]{1,0:T(8,128)(2,1)} %param.10) | copy-start | bytes 3538948
  6.5 199.6 %all-reduce.3.cloned.1.call-start = ((), (), s32[]{:S(2)}) async-start(), calls=%async_computation.4 | async-start | bytes 6291456 | tf_op jit(solution)/shard_map/psum | solution.py:66
  40.1 2.5 copy-start.3
  209.9 2.9 copy-start.2
  209.9 2.9 copy-start.4
  212.8 8.0 %copy-start.1 = (bf16[256,768]{1,0:T(8,128)(2,1)S(1)}, bf16[256,768]{1,0:T(8,128)(2,1)}, u32[]{:S(2)}) copy-start(bf16[256,768]{1,0:T(8,128)(2,1)} %param.11) | copy-start | bytes 1179652
  250.7 26.2 %copy-start.5 = (bf16[768,256]{1,0:T(8,128)(2,1)S(1)}, bf16[768,256]{1,0:T(8,128)(2,1)}, u32[]{:S(2)}) copy-start(bf16[768,256]{1,0:T(8,128)(2,1)} %param.13) | copy-start | bytes 1179652
  308.3 18.2 %collective-permute-start = (bf16[64,256]{1,0:T(8,128)(2,1)S(1)}, bf16[64,256]{1,0:T(8,128)(2,1)S(1)}, u32[]{:S(2)}, u32[]{:S(2)}) collective-permute-start(bf16[64,256]{1,0:T(8,128)(2,1)S(1)} %get-tuple-element.10), channel_id=1, source_target_pairs={{0,8},{1,24},{2,40},{3,56},{4,72},{5,88},{6,104},{7,120},{16,9},{1... | collective-permute-start | bytes 98312 | tf_op jit(solution)/shard_map/ppermute | solution.py:98
  316.5 16.9 %collective-permute-start.1 = (bf16[64,256]{1,0:T(8,128)(2,1)S(1)}, bf16[64,256]{1,0:T(8,128)(2,1)S(1)}, u32[]{:S(2)}, u32[]{:S(2)}) collective-permute-start(bf16[64,256]{1,0:T(8,128)(2,1)S(1)} %get-tuple-element.9), channel_id=1, source_target_pairs={{0,0},{1,16},{2,32},{3,48},{4,64},{5,80},{6,96},{7,112},{16,1},{17... | collective-permute-start | bytes 98312 | tf_op jit(solution)/shard_map/ppermute | solution.py:98
  324.5 8.9 %collective-permute-start.2 = (bf16[64,256]{1,0:T(8,128)(2,1)S(1)}, bf16[64,256]{1,0:T(8,128)(2,1)S(1)}, u32[]{:S(2)}, u32[]{:S(2)}) collective-permute-start(bf16[64,256]{1,0:T(8,128)(2,1)S(1)} %get-tuple-element.10), channel_id=1, source_target_pairs={{8,8},{9,24},{10,40},{11,56},{12,72},{13,88},{14,104},{15,120},{24... | collective-permute-start | bytes 98312 | tf_op jit(solution)/shard_map/ppermute | solution.py:98
  325.2 16.6 %collective-permute-start.3 = (bf16[64,256]{1,0:T(8,128)(2,1)S(1)}, bf16[64,256]{1,0:T(8,128)(2,1)S(1)}, u32[]{:S(2)}, u32[]{:S(2)}) collective-permute-start(bf16[64,256]{1,0:T(8,128)(2,1)S(1)} %get-tuple-element.9), channel_id=1, source_target_pairs={{8,0},{9,16},{10,32},{11,48},{12,64},{13,80},{14,96},{15,112},{24,... | collective-permute-start | bytes 98312 | tf_op jit(solution)/shard_map/ppermute | solution.py:98
Sparse Core Ops, SparseCore 0:
  45.4 160.6 all-reduce.2

commit v3 on v2

--- a/solution.py
+++ b/solution.py
@@ -63,7 +63,10 @@
     hidden_part = jnp.dot(flat_rows, vit_in, preferred_element_type=jnp.float32).astype(
         jnp.bfloat16
     )
+    qkv_part, hidden_part, proj_source = lax.optimization_barrier((qkv_part, hidden_part, proj))
     qkv_sum, hidden_sum = lax.psum((qkv_part, hidden_part), "narrow")
+    proj_all = gather_wide(proj_source, n_wide)
+    qkv_sum, hidden_sum, proj_all = lax.optimization_barrier((qkv_sum, hidden_sum, proj_all))
     qkv_all = qkv_sum.reshape(row_count, images, 3, heads_here, head_width)
     activated = jax.nn.gelu(hidden_sum.astype(jnp.float32), approximate=False).astype(
         jnp.bfloat16
@@ -80,26 +83,15 @@
     vit_output = (
         own_columns.reshape(flat_local, feature_block).astype(jnp.float32) + branch_sum
     ).astype(jnp.bfloat16)
-    output_rows = gather_wide(vit_output, n_wide)
-    partial_encoded = jnp.dot(output_rows, proj, preferred_element_type=jnp.float32)
-    encoded_piece = scatter_sum(partial_encoded, "narrow", n_narrow).astype(jnp.bfloat16)
-    ratio = n_wide // n_narrow
-    enc_block = proj.shape[1]
-    pieces = encoded_piece.reshape(ratio, flat_local, enc_block)
-    columns = []
-    for i in range(ratio):
-        got = None
-        for j in range(ratio):
-            pairs = [
-                (src_w * n_narrow + src_n, (ratio * src_n + j) * n_narrow + src_w // ratio)
-                for src_w in range(i, n_wide, ratio)
-                for src_n in range(n_narrow)
-            ]
-            moved = lax.ppermute(pieces[j], ("wide", "narrow"), pairs)
-            got = moved if got is None else jnp.where(w % ratio == j, moved, got)
-        columns.append(got)
-    encoded = jnp.concatenate(columns, axis=1)
-    return encoded.reshape(local_rows, images, ratio * enc_block)
+    proj_all = proj_all.reshape(n_wide, feature_block, proj.shape[1])
+    partial_encoded = jnp.einsum(
+        "rf,wfc->rwc", vit_output, proj_all, preferred_element_type=jnp.float32
+    ).astype(jnp.bfloat16)
+    partial_encoded = partial_encoded.reshape(flat_local, n_wide * proj.shape[1])
+    got = lax.all_to_all(partial_encoded, "narrow", 1, 0, tiled=True)
+    got = got.reshape(n_narrow, flat_local, -1)
+    encoded = jnp.sum(got.astype(jnp.float32), axis=0).astype(jnp.bfloat16)
+    return encoded.reshape(local_rows, images, -1)
 
 
 def solution(mesh):

time: 350 us -> 314 us (0.90)
  blocking collectives: 114 us -> 90.3 us
  starting transfers between devices: 18.1 us -> 4.85 us
  waiting for transfers between devices: 176 us -> 168 us
  local copies, waits for them, and re-layouts: 1.1 us -> 4.84 us
  matrix products: 19.6 us -> 23.2 us
    all_to_all x0 -> x1, blocking collectives: none -> 31.5 us  [per_device(): got = lax.all_to_all(partial_encoded, 'narrow', 1, 0, tiled=True)]
    all_to_all x2 -> x1, blocking collectives: 59.9 us -> 29.2 us  [scatter_sum(): lax.all_to_all(terms.astype(jnp.bfloat16), axis_name, 0, 0, tiled=True)]
    all_to_all x2 -> x1, blocking collectives: 54.5 us -> 29.6 us  [gather_wide(): got = lax.all_to_all(spread, 'wide', 0, 0, tiled=True)]
    ppermute x4 -> x0, starting transfers between devices: 18.1 us -> none  [per_device(): moved = lax.ppermute(pieces[j], ('wide', 'narrow'), pairs)]
    ppermute x4 -> x0, waiting for transfers between devices: 15.3 us -> none  [per_device(): moved = lax.ppermute(pieces[j], ('wide', 'narrow'), pairs)]
    psum x1, waiting for transfers between devices: 161 us -> 168 us  [per_device(): qkv_sum, hidden_sum = lax.psum((qkv_part, hidden_part), 'narrow')]
    all_to_all x0 -> x1, starting transfers between devices: none -> 4.63 us  [gather_wide(): got = lax.all_to_all(spread, 'wide', 0, 0, tiled=True)]
  transfers between devices with their start and end apart: 5 -> 2, of which waited for: 3 -> 1; matrix products, arithmetic and copies ran while one was open for 0% -> 0% of each run, Pallas kernels for 0% -> 0%
where the time goes in v3:
time: 314 us; the launch traced here: 310 us
  waiting for transfers between devices  168 us (54%)
  blocking collectives  90.3 us (29%)
  matrix products  23.2 us (7%)
  between operations  13.5 us (4%)
  other arithmetic  5.34 us (2%)
  starting transfers between devices  4.85 us (2%)
  local copies, waits for them, and re-layouts  4.84 us (2%)
    psum x1, waiting for transfers between devices, per_device(): qkv_sum, hidden_sum = lax.psum((qkv_part, hidden_part), 'narrow')  168 us
    all_to_all x1, blocking collectives, per_device(): got = lax.all_to_all(partial_encoded, 'narrow', 1, 0, tiled=True)  31.5 us
    all_to_all x1, blocking collectives, gather_wide(): got = lax.all_to_all(spread, 'wide', 0, 0, tiled=True)  29.6 us
    all_to_all x1, blocking collectives, scatter_sum(): lax.all_to_all(terms.astype(jnp.bfloat16), axis_name, 0, 0, tiled=True)  29.2 us
    dot_general x1, matrix products, per_device(): jnp.dot(units_rows, vit_mlp_out, preferred_element_type=jnp.float32)  8.08 us
  transfers between devices with their start and end apart: 2, of which 1 were waited for; matrix products, arithmetic and copies ran while one was open for 0% of the time, Pallas kernels for 0%

profile of v3, /device:TPU:480, one launch (start us, length us, event | category | flops | bytes accessed | tf_op | source)
XLA Modules:
  0.0 310.3 jit_solution(13277645347993730260)
XLA Ops:
  6.5 0.0 copy-start
  6.5 1.4 convert_reduce_fusion.1
  8.0 1.5 multiply_reduce_fusion.1
  9.5 0.8 dynamic-slice
  10.3 0.1 fusion.81
  10.4 0.1 broadcast_in_dim.7
  10.5 29.6 %all_to_all.32 = bf16[16,64,768]{2,1,0:T(8,128)(2,1)S(1)} all-to-all(bf16[16,64,768]{2,1,0:T(8,128)(2,1)S(1)} %broadcast_in_dim.7), channel_id=1, replica_groups=mesh['dp'=4,'wide'=16,'narrow'=8] {'wide'}, dimensions={0} | all-to-all | bytes 3145728 | tf_op jit(solution)/shard_map/all_to_all | solution.py:34
  40.1 0.0 copy-done
  40.1 0.0 copy-start.4
  40.1 2.5 convolution_convert_fusion
  42.7 0.0 copy-done.4
  42.7 0.0 copy-start.1
  42.7 2.6 convolution_convert_fusion.1
  45.3 0.0 copy-done.1
  45.3 3.3 %broadcast_in_dim.8 = bf16[16,768,256]{2,1,0:T(8,128)(2,1)} broadcast(bf16[768,256]{1,0:T(8,128)(2,1)S(1)} %copy-done.1), dimensions={1,2} | broadcast | bytes 6684672 | tf_op jit(solution)/shard_map/broadcast_in_dim | solution.py:33
  48.5 4.6 %all-to-all-start.1 = ((bf16[16,768,256]{2,1,0:T(8,128)(2,1)}), bf16[16,768,256]{2,1,0:T(8,128)(2,1)}, u32[]{:S(2)}, u32[]{:S(2)}) async-start(bf16[16,768,256]{2,1,0:T(8,128)(2,1)} %broadcast_in_dim.8), calls=%async_computation.1 | async-start | bytes 12582912 | tf_op jit(solution)/shard_map/all_to_all | solution.py:34
  53.2 0.2 all-reduce.3.cloned.1.call-start
  53.4 0.5 all-reduce.3.cloned.1.call-update
  53.9 167.7 %all-reduce.3.cloned.1.call-done = (bf16[1024,3,2,128]{3,0,2,1:T(8,128)(2,1)}, bf16[1024,768]{1,0:T(8,128)(2,1)}) async-done(((bf16[1024,3,2,128]{3,0,2,1:T(8,128)(2,1)}, bf16[1024,768]{1,0:T(8,128)(2,1)}), (bf16[1024,3,2,128]{3,0,2,1:T(8,128)(2,1)}, bf16[1024,768]{1,0:T(8,128)(2,1)})) %all-reduce.3.cloned.1.call-update) | async-done | bytes 3145744 | tf_op jit(solution)/shard_map/psum | solution.py:67
  221.6 0.0 all-to-all-done.1
  221.6 2.5 multiply_reduce_fusion
  224.1 1.4 fusion
  225.5 0.0 copy-start.3
  225.5 0.0 copy-start.5
  225.5 2.8 divide_convert_fusion
  228.4 0.0 copy-done.3
  228.4 0.0 copy-done.5
  228.4 0.0 copy-start.2
  228.4 8.1 %fusion.37 = f32[1024,768]{1,0:T(8,128)S(1)} fusion(bf16[768,768]{1,0:T(8,128)(2,1)S(1)} %copy-done.5, bf16[1024,768]{1,0:T(8,128)(2,1)S(1)} %copy-done.3), kind=kOutput, calls=%fused_computation.47 | convolution fusion | flops 1259864064 | bytes 5898240 | tf_op jit(solution)/shard_map/dot_general | solution.py:78
  236.5 0.0 copy-done.2
  236.5 0.6 add_convert_fusion
  237.1 29.2 %all_to_all.33 = bf16[16,64,768]{2,1,0:T(8,128)(2,1)S(1)} all-to-all(bf16[16,64,768]{2,1,0:T(8,128)(2,1)S(1)} %bitcast.55), channel_id=1, replica_groups=mesh['dp'=4,'wide'=16,'narrow'=8] {'wide'}, dimensions={0} | all-to-all | bytes 3145728 | tf_op jit(solution)/shard_map/all_to_all | solution.py:39
  266.3 0.2 convert_reduce_fusion
  266.6 4.0 %convolution_convert_fusion.2 = bf16[64,16,256]{2,0,1:T(8,128)(2,1)S(1)} fusion(bf16[16,768,256]{2,1,0:T(8,128)(2,1)} %bitcast.19, f32[64,768]{1,0:T(8,128)S(1)} %convert_reduce_fusion, bf16[64,1,6144]{2,0,1:T(8,128)(2,1)} %param.7, s32[]{:T(128)S(6)} %select_n.4), kind=kOutput, calls=%fused_computation.80 | convolution fusion | flops 403062784 | bytes 7110660 | tf_op jit(solution)/shard_map/rf,wfc->rwc/dot_general | solution.py:87
  270.6 0.3 copy.18
  270.9 0.2 all_to_all.26
  271.1 0.2 copy.19
  271.3 31.5 %all_to_all.34 = bf16[64,8,512]{2,0,1:T(8,128)(2,1)S(1)} all-to-all(bf16[64,8,512]{2,0,1:T(8,128)(2,1)S(1)} %copy.19), channel_id=1, replica_groups=mesh['dp'=4,'wide'=16,'narrow'=8] {'narrow'}, dimensions={1} | all-to-all | bytes 1048576 | tf_op jit(solution)/shard_map/all_to_all | solution.py:91
  302.8 0.7 reduce_sum.58
  (2 shorter events, 0.0 us)
Async XLA Ops:
  6.5 33.6 %copy-start = (bf16[768,768]{1,0:T(8,128)(2,1)S(1)}, bf16[768,768]{1,0:T(8,128)(2,1)}, u32[]{:S(2)}) copy-start(bf16[768,768]{1,0:T(8,128)(2,1)} %param.10) | copy-start | bytes 3538948
  40.1 2.5 copy-start.4
  42.7 2.6 copy-start.1
  48.5 173.1 %all-to-all-start.1 = ((bf16[16,768,256]{2,1,0:T(8,128)(2,1)}), bf16[16,768,256]{2,1,0:T(8,128)(2,1)}, u32[]{:S(2)}, u32[]{:S(2)}) async-start(bf16[16,768,256]{2,1,0:T(8,128)(2,1)} %broadcast_in_dim.8), calls=%async_computation.1 | async-start | bytes 12582912 | tf_op jit(solution)/shard_map/all_to_all | solution.py:34
  53.2 168.5 %all-reduce.3.cloned.1.call-start = ((), (), s32[]{:S(2)}) async-start(), calls=%async_computation.4 | async-start | bytes 6291456 | tf_op jit(solution)/shard_map/psum | solution.py:67
  225.5 2.9 copy-start.3
  225.5 2.9 copy-start.5
  228.4 8.1 %copy-start.2 = (bf16[256,768]{1,0:T(8,128)(2,1)S(1)}, bf16[256,768]{1,0:T(8,128)(2,1)}, u32[]{:S(2)}) copy-start(bf16[256,768]{1,0:T(8,128)(2,1)} %param.11) | copy-start | bytes 1179652
Sparse Core Ops, SparseCore 0:
  57.0 164.5 all-reduce.2

commit v4 on v3

--- a/solution.py
+++ b/solution.py
@@ -71,6 +71,7 @@
     activated = jax.nn.gelu(hidden_sum.astype(jnp.float32), approximate=False).astype(
         jnp.bfloat16
     )
+    activated = lax.optimization_barrier(activated)
     mixed_heads = attend(qkv_all[:, :, 0], qkv_all[:, :, 1], qkv_all[:, :, 2])
     heads_rows = mixed_heads.reshape(row_count * images, heads_here * head_width)
     units_rows = activated.reshape(row_count * images, -1)

time: 314 us -> 314 us (level)
  other arithmetic: 5.34 us -> 12.2 us
  matrix products: 23.2 us -> 16.5 us
    convert_element_type x0 -> x1, other arithmetic: none -> 6.9 us  [per_device(): jax.nn.gelu(hidden_sum.astype(jnp.float32), approximate=False)]
    dot_general x1, matrix products: 8.08 us -> 1.39 us  [per_device(): jnp.dot(units_rows, vit_mlp_out, preferred_element_type=jnp.float32)]
where the time goes in v4:
time: 314 us; the launch traced here: 311 us
  waiting for transfers between devices  168 us (54%)
  blocking collectives  90.3 us (29%)
  matrix products  16.5 us (5%)
  between operations  13.6 us (4%)
  other arithmetic  12.2 us (4%)
  local copies, waits for them, and re-layouts  4.84 us (2%)
  starting transfers between devices  4.67 us (1%)
    psum x1, waiting for transfers between devices, per_device(): qkv_sum, hidden_sum = lax.psum((qkv_part, hidden_part), 'narrow')  168 us
    all_to_all x1, blocking collectives, per_device(): got = lax.all_to_all(partial_encoded, 'narrow', 1, 0, tiled=True)  31.5 us
    all_to_all x1, blocking collectives, gather_wide(): got = lax.all_to_all(spread, 'wide', 0, 0, tiled=True)  29.6 us
    all_to_all x1, blocking collectives, scatter_sum(): lax.all_to_all(terms.astype(jnp.bfloat16), axis_name, 0, 0, tiled=True)  29.2 us
    convert_element_type x1, other arithmetic, per_device(): jax.nn.gelu(hidden_sum.astype(jnp.float32), approximate=False)  6.9 us
  transfers between devices with their start and end apart: 2, of which 1 were waited for; matrix products, arithmetic and copies ran while one was open for 0% of the time, Pallas kernels for 0%

profile of v4, /device:TPU:480, one launch (start us, length us, event | category | flops | bytes accessed | tf_op | source)
XLA Modules:
  0.0 310.5 jit_solution(8520701258002110065)
XLA Ops:
  6.5 0.0 copy-start
  6.5 1.4 convert_reduce_fusion.1
  8.0 1.5 multiply_reduce_fusion.1
  9.5 0.8 dynamic-slice
  10.3 0.1 fusion.49
  10.4 0.1 broadcast_in_dim.7
  10.5 29.6 %all_to_all.32 = bf16[16,64,768]{2,1,0:T(8,128)(2,1)S(1)} all-to-all(bf16[16,64,768]{2,1,0:T(8,128)(2,1)S(1)} %broadcast_in_dim.7), channel_id=1, replica_groups=mesh['dp'=4,'wide'=16,'narrow'=8] {'wide'}, dimensions={0} | all-to-all | bytes 3145728 | tf_op jit(solution)/shard_map/all_to_all | solution.py:34
  40.1 0.0 copy-done
  40.1 0.0 copy-start.4
  40.1 2.5 convolution_convert_fusion
  42.7 0.0 copy-done.4
  42.7 0.0 copy-start.2
  42.7 2.6 convolution_convert_fusion.1
  45.3 0.0 copy-done.2
  45.3 3.3 %broadcast_in_dim.8 = bf16[16,768,256]{2,1,0:T(8,128)(2,1)} broadcast(bf16[768,256]{1,0:T(8,128)(2,1)S(1)} %copy-done.2), dimensions={1,2} | broadcast | bytes 6684672 | tf_op jit(solution)/shard_map/broadcast_in_dim | solution.py:33
  48.5 4.6 %all-to-all-start.1 = ((bf16[16,768,256]{2,1,0:T(8,128)(2,1)}), bf16[16,768,256]{2,1,0:T(8,128)(2,1)}, u32[]{:S(2)}, u32[]{:S(2)}) async-start(bf16[16,768,256]{2,1,0:T(8,128)(2,1)} %broadcast_in_dim.8), calls=%async_computation.1 | async-start | bytes 12582912 | tf_op jit(solution)/shard_map/all_to_all | solution.py:34
  53.2 0.0 all-reduce.3.cloned.1.call-start
  53.2 0.7 all-reduce.3.cloned.1.call-update
  53.9 167.7 %all-reduce.3.cloned.1.call-done = (bf16[1024,3,2,128]{3,0,2,1:T(8,128)(2,1)}, bf16[1024,768]{1,0:T(8,128)(2,1)}) async-done(((bf16[1024,3,2,128]{3,0,2,1:T(8,128)(2,1)}, bf16[1024,768]{1,0:T(8,128)(2,1)}), (bf16[1024,3,2,128]{3,0,2,1:T(8,128)(2,1)}, bf16[1024,768]{1,0:T(8,128)(2,1)})) %all-reduce.3.cloned.1.call-update) | async-done | bytes 3145744 | tf_op jit(solution)/shard_map/psum | solution.py:67
  221.6 0.0 all-to-all-done.1
  221.6 2.5 multiply_reduce_fusion
  224.1 1.4 fusion
  225.5 0.0 copy-start.1
  225.5 2.8 divide_convert_fusion
  228.3 0.0 copy-done.1
  228.3 0.0 copy-start.5
  228.3 6.9 %fusion.7 = bf16[1024,768]{1,0:T(8,128)(2,1)S(1)} fusion(bf16[1024,768]{1,0:T(8,128)(2,1)S(1)} %copy-done.1), kind=kLoop, calls=%fused_computation.11 | loop fusion | flops 51904512 | bytes 3145728 | tf_op jit(solution)/shard_map/convert_element_type | solution.py:71
  235.2 0.0 copy-done.5
  235.2 0.0 copy-start.3
  235.2 1.4 fusion.53
  236.6 0.0 copy-done.3
  236.6 0.6 add_convert_fusion
  237.3 29.2 %all_to_all.33 = bf16[16,64,768]{2,1,0:T(8,128)(2,1)S(1)} all-to-all(bf16[16,64,768]{2,1,0:T(8,128)(2,1)S(1)} %bitcast.56), channel_id=1, replica_groups=mesh['dp'=4,'wide'=16,'narrow'=8] {'wide'}, dimensions={0} | all-to-all | bytes 3145728 | tf_op jit(solution)/shard_map/all_to_all | solution.py:39
  266.5 0.2 convert_reduce_fusion
  266.7 4.0 %convolution_convert_fusion.2 = bf16[64,16,256]{2,0,1:T(8,128)(2,1)S(1)} fusion(bf16[16,768,256]{2,1,0:T(8,128)(2,1)} %bitcast.19, f32[64,768]{1,0:T(8,128)S(1)} %convert_reduce_fusion, bf16[64,1,6144]{2,0,1:T(8,128)(2,1)} %param.7, s32[]{:T(128)S(6)} %select_n.4), kind=kOutput, calls=%fused_computation.49 | convolution fusion | flops 403062784 | bytes 7110660 | tf_op jit(solution)/shard_map/rf,wfc->rwc/dot_general | solution.py:88
  270.8 0.3 copy.18
  271.1 0.2 all_to_all.26
  271.3 0.2 copy.19
  271.4 31.5 %all_to_all.34 = bf16[64,8,512]{2,0,1:T(8,128)(2,1)S(1)} all-to-all(bf16[64,8,512]{2,0,1:T(8,128)(2,1)S(1)} %copy.19), channel_id=1, replica_groups=mesh['dp'=4,'wide'=16,'narrow'=8] {'narrow'}, dimensions={1} | all-to-all | bytes 1048576 | tf_op jit(solution)/shard_map/all_to_all | solution.py:92
  303.0 0.7 reduce_sum.58
  (2 shorter events, 0.0 us)
Async XLA Ops:
  6.5 33.6 %copy-start = (bf16[768,768]{1,0:T(8,128)(2,1)S(1)}, bf16[768,768]{1,0:T(8,128)(2,1)}, u32[]{:S(2)}) copy-start(bf16[768,768]{1,0:T(8,128)(2,1)} %param.10) | copy-start | bytes 3538948
  40.1 2.5 copy-start.4
  42.7 2.6 copy-start.2
  48.5 173.1 %all-to-all-start.1 = ((bf16[16,768,256]{2,1,0:T(8,128)(2,1)}), bf16[16,768,256]{2,1,0:T(8,128)(2,1)}, u32[]{:S(2)}, u32[]{:S(2)}) async-start(bf16[16,768,256]{2,1,0:T(8,128)(2,1)} %broadcast_in_dim.8), calls=%async_computation.1 | async-start | bytes 12582912 | tf_op jit(solution)/shard_map/all_to_all | solution.py:34
  53.2 168.4 %all-reduce.3.cloned.1.call-start = ((), (), s32[]{:S(2)}) async-start(), calls=%async_computation.4 | async-start | bytes 6291456 | tf_op jit(solution)/shard_map/psum | solution.py:67
  225.5 2.8 copy-start.1
  228.3 6.9 %copy-start.5 = (bf16[768,768]{1,0:T(8,128)(2,1)S(1)}, bf16[768,768]{1,0:T(8,128)(2,1)}, u32[]{:S(2)}) copy-start(bf16[768,768]{1,0:T(8,128)(2,1)} %param.12) | copy-start | bytes 3538948
  235.2 1.4 copy-start.3
Sparse Core Ops, SparseCore 0:
  57.0 164.5 all-reduce.2
